TPU v7x, 32 devices: a whole 2x2x4 slice. The times are simulated.
32 devices in a mesh: group: 2 (over y), tm: 4 (over z), member: 2 (over x), sub: 2 (over core).
Axes of the slice: x: 2, y: 2, z: 4, core: 2. Of those that a mesh axis runs over, the one named last changes fastest.
Arguments:
- slices: float32 [8, 4, 2, 256, 256], P(('group', 'member', 'sub'), 'tm'), parts along dimension 0, may hold values from -1 to 1, as said below
- controls: float32 [4, 2, 256, 256], replicated, as said below
- target: float32 [4, 256, 256], P('group'), parts along dimension 0, may hold values from -1 to 1, as said below
Outputs:
- gradient: float32 [8, 4], P(('group', 'tm')), parts along dimension 0
There are 2 independent parts, one for each index of `group`. A program takes and returns all parts, laid end to end along the dimension named above; an argument that names none is the same for every part. Nothing has to cross between parts.
Inputs may be any that keep to these rules, and one draw needn't show every extreme that they name: Each slices[m, k] is a unitary matrix. `controls`: each control generator is Hermitian. The target is a unitary matrix.
All inputs are finite; a program needn't handle non-finite values.
Results may differ from a plain program's by a relative error of at most 0.0003.
Values sent between devices are 32-bit elements; how exact they have to be, the bound alone decides.
No kernel may reach another device: no remote copies, remote signals or barrier semaphores. Data moves between devices by JAX's collectives and lax.ppermute only.
A program may use at most 64 MiB of HBM per device.

v0:
```python
import jax
import jax.numpy as jnp
from jax import lax
from jax.sharding import PartitionSpec as P

HIGH = lax.Precision.HIGHEST


def cmul(left, right):
    real_part = jnp.matmul(left[..., 0, :, :], right[..., 0, :, :], precision=HIGH) - jnp.matmul(
        left[..., 1, :, :], right[..., 1, :, :], precision=HIGH
    )
    imag_part = jnp.matmul(left[..., 0, :, :], right[..., 1, :, :], precision=HIGH) + jnp.matmul(
        left[..., 1, :, :], right[..., 0, :, :], precision=HIGH
    )
    return jnp.stack([real_part, imag_part], axis=-3)


def cdagger(matrix):
    return jnp.stack(
        [jnp.swapaxes(matrix[..., 0, :, :], -1, -2), -jnp.swapaxes(matrix[..., 1, :, :], -1, -2)],
        axis=-3,
    )


def local_suffixes(identity_b):
    pieces = [identity_b]
    return jnp.stack(pieces, axis=1)


def tree_product(matrices):
    while matrices.shape[0] > 1:
        earlier_half = matrices[0::2]
        later_half = matrices[1::2]
        matrices = cmul(later_half, earlier_half)
    return matrices[0]


def per_device(slices, controls, target):
    members_here = slices.shape[0]
    order = slices.shape[-1]
    identity = jnp.stack(
        [jnp.eye(order, dtype=jnp.float32), jnp.zeros((order, order), jnp.float32)]
    )
    identity_b = jnp.broadcast_to(identity, (members_here, 2, order, order))
    target_dag = cdagger(target)
    current = slices[:, 0]
    prefixes = [current]
    local_prefix = jnp.stack(prefixes, axis=1)
    blocks = lax.axis_size("tm")
    position = lax.axis_index("tm")
    gathered = lax.all_gather(current, "tm", axis=0, tiled=True)
    gathered = gathered.reshape((blocks, members_here, 2, order, order))
    block_ids = jnp.arange(blocks, dtype=jnp.int32)[:, None, None, None, None]
    early_set = jnp.where(block_ids < position, gathered, identity_b[None])
    late_set = jnp.where(block_ids > position, gathered, identity_b[None])
    carry_in = tree_product(early_set)
    carry_out = tree_product(late_set)
    forward = cmul(local_prefix, carry_in[:, None])
    backward = cmul(carry_out[:, None], local_suffixes(identity_b))
    costate = cmul(cmul(forward, target_dag), backward)
    over_re = jnp.trace(costate[:, 0, 0], axis1=-2, axis2=-1)
    over_im = jnp.trace(costate[:, 0, 1], axis1=-2, axis2=-1)
    s_re = jnp.einsum(
        "mkab,jab->mkj", costate[:, :, 0], controls[:, 0], precision=HIGH
    ) + jnp.einsum("mkab,jab->mkj", costate[:, :, 1], controls[:, 1], precision=HIGH)
    s_im = jnp.einsum(
        "mkab,jab->mkj", costate[:, :, 1], controls[:, 0], precision=HIGH
    ) - jnp.einsum("mkab,jab->mkj", costate[:, :, 0], controls[:, 1], precision=HIGH)
    terms = over_re[:, None, None] * s_im - over_im[:, None, None] * s_re
    partial_value = jnp.sum(terms, axis=0)
    total = lax.psum(partial_value, ("member", "sub"))
    member_count = members_here * lax.axis_size("member") * lax.axis_size("sub")
    return total * (2.0 / member_count)


def solution(mesh):
    placed = (P(("group", "member", "sub"), "tm", None, None, None), P(), P("group", None, None))
    return jax.shard_map(
        per_device, mesh=mesh, in_specs=placed, out_specs=P(("group", "tm"), None), check_vma=False
    )
```

profile of v0, /device:TPU:0, one launch (start us, length us, event | category | flops | bytes accessed | tf_op | source)
XLA Modules:
  0.0 112.9 jit_solution(17755203991981334427)
XLA Ops:
  6.5 0.0 all-gather.3.cloned.1.call-start
  6.5 0.7 all-gather.3.cloned.1.call-update
  7.3 0.1 pad_bitcast_fusion
  7.4 1.8 %slice_bitcast_fusion.1 = (f32[4,256,256]{2,1,0:T(8,128)S(1)}, f32[4,256,256]{2,1,0:T(8,128)S(1)}) fusion(f32[4,2,256,256]{3,2,1,0:T(8,128)} %param.4), kind=kLoop, calls=%fused_computation.31 | loop fusion | bytes 4194304 | tf_op jit(solution)/shard_map/squeeze | solution.py:68
  9.2 48.4 %all-gather.3.cloned.1.call-done = f32[4,1,2,256,256]{4,3,0,2,1:T(8,128)} async-done(((f32[1,1,2,256,256]{4,3,0,2,1:T(8,128)}), f32[4,1,2,256,256]{4,3,0,2,1:T(8,128)}) %all-gather.3.cloned.1.call-update) | async-done | bytes 2097168 | tf_op jit(solution)/shard_map/all_gather | solution.py:52
  57.6 2.1 %fusion.1 = (f32[4,1,2,256,256]{4,3,0,2,1:T(8,128)S(1)}, f32[4,1,2,256,256]{4,3,0,2,1:T(8,128)S(1)}) fusion(f32[4,1,2,256,256]{4,3,0,2,1:T(8,128)} %all-gather.3.cloned.1.call-done, f32[2,256,256]{2,1,0:T(8,128)S(1)} %get-tuple-element.14, pred[4]{0:T(512)(128)(4,1)S(1)} %get-tuple-element.19, pred[4]{0:T(512)(128)(4,1)S(1)} %get-tuple-element.20), kind=kLoop, calls=%fused_computation.3 | loop fusion | flops 1048576 | bytes 6815752 | tf_op jit(solution)/shard_map/jit(_where)/select_n | solution.py:56
  59.7 0.2 fusion.44
  59.9 0.7 fusion.14
  60.6 0.7 fusion.15
  61.2 0.7 convolution_add_fusion
  61.9 0.7 convolution_subtract_fusion
  62.6 0.4 fusion.31
  62.9 0.4 fusion.30
  63.3 0.4 convolution_subtract_fusion.4
  63.7 0.3 fusion.39
  64.0 0.3 fusion.38
  64.3 0.2 fusion.45
  64.5 0.7 fusion.12
  65.2 0.7 fusion.13
  65.9 0.7 convolution_add_fusion.1
  66.5 0.7 convolution_subtract_fusion.1
  67.2 0.0 copy-start
  67.2 0.4 fusion.29
  67.6 0.4 fusion.28
  68.0 0.4 convolution_add_fusion.7
  68.4 0.0 copy-start.1
  68.4 0.4 convolution_subtract_fusion.7
  68.8 0.0 copy-done
  68.8 0.6 fusion.26
  69.4 0.6 fusion.24
  70.0 0.6 convolution_subtract_fusion.6
  70.6 0.0 copy-done.1
  70.6 0.6 fusion.16
  71.2 0.8 fusion.20
  72.0 0.4 convolution_add_fusion.5
  72.4 0.3 convolution_add_fusion.3
  72.7 0.3 convolution_subtract_fusion.3
  73.0 0.6 convolution_add_fusion.6
  73.6 0.6 convolution_add_fusion.4
  74.2 0.6 convolution_subtract_fusion.5
  74.8 0.4 fusion.47
  75.2 0.4 fusion.46
  75.6 1.0 select_reduce_fusion
  76.5 1.0 select_reduce_fusion.1
  77.5 5.0 %convolution_bitcast_fusion = f32[4]{0:T(128)S(1)} fusion(f32[4,256,256]{2,1,0:T(8,128)S(1)} %get-tuple-element.8, f32[256,256,1]{1,0,2:T(8,128)S(1)} %bitcast.155), kind=kOutput, calls=%fused_computation.20 | convolution fusion | flops 3145728 | bytes 1310736 | tf_op jit(solution)/shard_map/mkab,jab->mkj/dot_general | solution.py:66
  82.5 5.0 %convolution_bitcast_fusion.2 = f32[4]{0:T(128)S(1)} fusion(f32[4,256,256]{2,1,0:T(8,128)S(1)} %get-tuple-element.8, f32[256,256,1]{1,0,2:T(8,128)S(1)} %bitcast.157), kind=kOutput, calls=%fused_computation.22 | convolution fusion | flops 3145728 | bytes 1310736 | tf_op jit(solution)/shard_map/mkab,jab->mkj/dot_general | solution.py:69
  87.5 5.6 %fusion.7 = f32[4]{0:T(128)S(1)} fusion(f32[4]{0:T(128)S(1)} %convolution_bitcast_fusion, f32[4,256,256]{2,1,0:T(8,128)S(1)} %get-tuple-element.7, f32[256,256,1]{1,0,2:T(8,128)S(1)} %bitcast.158, f32[]{:T(128)} %get-tuple-element.15), kind=kOutput, calls=%fused_computation.29 | convolution fusion | flops 3145736 | bytes 1310756 | tf_op jit(solution)/shard_map/mkab,jab->mkj/dot_general | solution.py:64
  93.1 5.6 %fusion.5 = f32[1,4]{1,0:T(1,128)S(1)} fusion(f32[4]{0:T(128)S(1)} %fusion.7, f32[4]{0:T(128)S(1)} %convolution_bitcast_fusion.2, f32[4,256,256]{2,1,0:T(8,128)S(1)} %get-tuple-element.7, f32[256,256,1]{1,0,2:T(8,128)S(1)} %bitcast.156, f32[]{:T(128)} %get-tuple-element.17), kind=kOutput, calls=%fused_computation.27 | convolution fusion | flops 3145740 | bytes 1310772 | tf_op jit(solution)/shard_map/mkab,jab->mkj/dot_general | solution.py:67
  98.7 6.8 %psum.7 = f32[1,4]{1,0:T(1,128)S(1)} all-reduce(f32[1,4]{1,0:T(1,128)S(1)} %fusion.5), channel_id=1, replica_groups=mesh['group'=2,'tm'=4,'member'=2,'sub'=2] {'member','sub'}, use_global_device_ids=true, to_apply=%region_2.3 | all-reduce | flops 4 | bytes 32 | tf_op jit(solution)/shard_map/psum | solution.py:72
  105.5 0.5 broadcast_multiply_fusion
  (2 shorter events, 0.0 us)
Async XLA Ops:
  6.5 51.1 %all-gather.3.cloned.1.call-start = ((), (), s32[]{:S(2)}) async-start(), calls=%async_computation | async-start | bytes 2621440 | tf_op jit(solution)/shard_map/all_gather | solution.py:52
  67.2 1.6 %copy-start = (f32[1,1,2,256,256]{4,3,2,1,0:T(8,128)S(1)}, f32[1,1,2,256,256]{4,3,2,1,0:T(8,128)}, u32[]{:S(2)}) copy-start(f32[1,1,2,256,256]{4,3,2,1,0:T(8,128)} %param.3) | copy-start | bytes 1572868
  68.4 2.2 %copy-start.1 = (f32[2,256,256]{2,1,0:T(8,128)S(1)}, f32[2,256,256]{2,1,0:T(8,128)}, u32[]{:S(2)}) copy-start(f32[2,256,256]{2,1,0:T(8,128)} %param.5) | copy-start | bytes 1572868
Sparse Core Ops, SparseCore 0:
  8.9 48.6 all-gather.2
where the time goes:
time: 113 us
  waiting for transfers between devices  49.1 us (43%)
  matrix products  38.3 us (34%)
  between operations  13.7 us (12%)
  blocking collectives  6.82 us (6%)
  other arithmetic  2.67 us (2%)
  local copies, waits for them, and re-layouts  2.22 us (2%)
    all_gather x1, waiting for transfers between devices, per_device(): gathered = lax.all_gather(current, 'tm', axis=0, tiled=True)  48.4 us
    psum x1, blocking collectives, per_device(): total = lax.psum(partial_value, ('member', 'sub'))  6.82 us
    dot_general x1, matrix products, per_device(): jnp.einsum('mkab,jab->mkj', costate[:, :, 1], controls[:, 0], precision=H...  5.59 us
    dot_general x1, matrix products, per_device(): jnp.einsum('mkab,jab->mkj', costate[:, :, 0], controls[:, 0], precision=H...  5.59 us
    dot_general x1, matrix products, per_device(): jnp.einsum('mkab,jab->mkj', costate[:, :, 0], controls[:, 1], precision=H...  4.99 us
    dot_general x1, matrix products, per_device(): jnp.einsum('mkab,jab->mkj', costate[:, :, 1], controls[:, 1], precision=H...  4.97 us
    dot_general x8, matrix products, cmul(): jnp.matmul(left[..., 1, :, :], right[..., 1, :, :], precision=HIGH)  4.55 us
    dot_general x8, matrix products, cmul(): jnp.matmul(left[..., 1, :, :], right[..., 0, :, :], precision=HIGH)  4.55 us
  transfers between devices with their start and end apart: 1, of which 1 were waited for; matrix products, arithmetic and copies ran while one was open for 2% of the time, Pallas kernels for 0%

commit v1 on v0

--- a/solution.py
+++ b/solution.py
@@ -49,7 +49,24 @@
     local_prefix = jnp.stack(prefixes, axis=1)
     blocks = lax.axis_size("tm")
     position = lax.axis_index("tm")
-    gathered = lax.all_gather(current, "tm", axis=0, tiled=True)
+    devices, position_2, extent = (lax.axis_size("tm"), lax.axis_index("tm"), current.shape[0])
+    forward_2 = [(i, (i + 1) % devices) for i in range(devices)]
+    behind = [(i, (i - 1) % devices) for i in range(devices)]
+    out = jnp.zeros((*current.shape[:0], devices * extent, *current.shape[0 + 1 :]), current.dtype)
+    out = lax.dynamic_update_slice_in_dim(out, current, position_2 * extent, axis=0)
+    from_left = from_right = current
+    half = devices // 2
+    for turn in range(1, half + 1):
+        from_left = lax.ppermute(from_left, "tm", forward_2)
+        out = lax.dynamic_update_slice_in_dim(
+            out, from_left, (position_2 - turn) % devices * extent, axis=0
+        )
+        if turn < devices - half:
+            from_right = lax.ppermute(from_right, "tm", behind)
+            out = lax.dynamic_update_slice_in_dim(
+                out, from_right, (position_2 + turn) % devices * extent, axis=0
+            )
+    gathered = out
     gathered = gathered.reshape((blocks, members_here, 2, order, order))
     block_ids = jnp.arange(blocks, dtype=jnp.int32)[:, None, None, None, None]
     early_set = jnp.where(block_ids < position, gathered, identity_b[None])

time: 113 us -> 90.8 us (0.80)
  waiting for transfers between devices: 49.1 us -> 31.5 us
  between operations: 13.7 us -> 0.36 us
  starting transfers between devices: 0.01 us -> 6.67 us
  local copies, waits for them, and re-layouts: 2.22 us -> 6.8 us
  other arithmetic: 2.67 us -> 1.08 us
  blocking collectives: 6.82 us -> 5.65 us
    all_gather x1 -> x0, waiting for transfers between devices: 48.4 us -> none  [per_device(): gathered = lax.all_gather(current, 'tm', axis=0, tiled=True)]
    ppermute x0 -> x3, waiting for transfers between devices: none -> 31.5 us  [the longest x2 31.5 us: per_device(): from_left = lax.ppermute(from_left, 'tm', forward_2)]
    ppermute x0 -> x3, starting transfers between devices: none -> 6.67 us  [the longest x1 5.05 us: per_device(): from_right = lax.ppermute(from_right, 'tm', behind)]
    dynamic_update_slice x0 -> x4, local copies, waits for them, and re-layouts: none -> 3.32 us  [the longest x2 2.19 us: per_device(): lax.dynamic_update_slice_in_dim(out, from_left, (position_2 - turn) % dev...]
    select_n x1, other arithmetic: 2.05 us -> 0.47 us  [per_device(): late_set = jnp.where(block_ids > position, gathered, identity_b[None])]
    unnamed x4 -> x10, local copies, waits for them, and re-layouts: 0.01 us -> 1.37 us
    psum x1, blocking collectives: 6.82 us -> 5.65 us  [per_device(): total = lax.psum(partial_value, ('member', 'sub'))]
  transfers between devices with their start and end apart: 1 -> 3, of which waited for: 1 -> 2; matrix products, arithmetic and copies ran while one was open for 2% -> 4% of each run, Pallas kernels for 0% -> 0%
where the time goes in v1:
time: 90.8 us; the launch traced here: 90.5 us
  matrix products  38.4 us (42%)
  waiting for transfers between devices  31.5 us (35%)
  local copies, waits for them, and re-layouts  6.8 us (7%)
  starting transfers between devices  6.67 us (7%)
  blocking collectives  5.65 us (6%)
  other arithmetic  1.08 us (1%)
    ppermute x2, waiting for transfers between devices, per_device(): from_left = lax.ppermute(from_left, 'tm', forward_2)  31.5 us
    dot_general x1, matrix products, per_device(): jnp.einsum('mkab,jab->mkj', costate[:, :, 1], controls[:, 0], precision=H...  5.65 us
    psum x1, blocking collectives, per_device(): total = lax.psum(partial_value, ('member', 'sub'))  5.65 us
    dot_general x1, matrix products, per_device(): jnp.einsum('mkab,jab->mkj', costate[:, :, 0], controls[:, 0], precision=H...  5.59 us
    ppermute x1, starting transfers between devices, per_device(): from_right = lax.ppermute(from_right, 'tm', behind)  5.05 us
    dot_general x1, matrix products, per_device(): jnp.einsum('mkab,jab->mkj', costate[:, :, 0], controls[:, 1], precision=H...  4.99 us
    dot_general x1, matrix products, per_device(): jnp.einsum('mkab,jab->mkj', costate[:, :, 1], controls[:, 1], precision=H...  4.97 us
    dot_general x8, matrix products, cmul(): jnp.matmul(left[..., 1, :, :], right[..., 1, :, :], precision=HIGH)  4.61 us
  transfers between devices with their start and end apart: 3, of which 2 were waited for; matrix products, arithmetic and copies ran while one was open for 4% of the time, Pallas kernels for 0%

profile of v1, /device:TPU:0, one launch (start us, length us, event | category | flops | bytes accessed | tf_op | source)
XLA Modules:
  0.0 90.5 jit_solution(85274664777565794)
XLA Ops:
  0.0 0.0 copy-start
  0.0 5.0 %collective-permute-start.1 = (f32[1,2,256,256]{3,2,1,0:T(8,128)}, f32[1,2,256,256]{3,2,1,0:T(8,128)}, u32[]{:S(2)}, u32[]{:S(2)}) collective-permute-start(f32[1,2,256,256]{3,2,1,0:T(8,128)} %bitcast.155), channel_id=1, source_target_pairs={{0,12},{4,0},{8,4},{12,8},{1,13},{5,1},{9,5},{13,9},{2,14},{6,2},{... | collective-permute-start | bytes 1572872 | tf_op jit(solution)/shard_map/ppermute | solution.py:65
  5.1 0.0 collective-permute-start
  5.1 0.0 copy-start.1
  5.1 0.2 reshape.151
  5.2 0.0 copy-done
  5.3 1.3 %copy-done.1 = f32[4,2,256,256]{3,2,1,0:T(8,128)S(1)} copy-done((f32[4,2,256,256]{3,2,1,0:T(8,128)S(1)}, f32[4,2,256,256]{3,2,1,0:T(8,128)}, u32[]{:S(2)}) %copy-start.1) | copy-done | bytes 2097176
  6.6 1.5 %slice_bitcast_fusion.1 = (f32[4,256,256]{2,1,0:T(8,128)}, f32[4,256,256]{2,1,0:T(8,128)}) fusion(f32[4,2,256,256]{3,2,1,0:T(8,128)S(1)} %copy-done.1), kind=kLoop, calls=%fused_computation.27 | loop fusion | bytes 4194304 | tf_op jit(solution)/shard_map/squeeze | solution.py:85
  8.2 0.1 pad_bitcast_fusion
  8.3 20.4 %collective-permute-done = f32[1,2,256,256]{3,2,1,0:T(8,128)} collective-permute-done((f32[1,2,256,256]{3,2,1,0:T(8,128)}, f32[1,2,256,256]{3,2,1,0:T(8,128)}, u32[]{:S(2)}, u32[]{:S(2)}) %collective-permute-start) | collective-permute-done | bytes 524320 | tf_op jit(solution)/shard_map/ppermute | solution.py:60
  28.7 1.6 %collective-permute-start.2 = (f32[1,2,256,256]{3,2,1,0:T(8,128)}, f32[1,2,256,256]{3,2,1,0:T(8,128)}, u32[]{:S(2)}, u32[]{:S(2)}) collective-permute-start(f32[1,2,256,256]{3,2,1,0:T(8,128)} %collective-permute-done), channel_id=1, source_target_pairs={{0,4},{4,8},{8,12},{12,0},{1,5},{5,9},{9,13},{13,1},{2,6},{6,10},{... | collective-permute-start | bytes 1572872 | tf_op jit(solution)/shard_map/ppermute | solution.py:60
  30.3 1.1 %bitcast_dynamic-update-slice_fusion.1 = f32[4,1,2,256,256]{4,3,0,2,1:T(8,128)S(1)} fusion(f32[4,1,2,256,256]{4,3,0,2,1:T(8,128)S(1)} %bitcast_dynamic-update-slice_fusion.3, s32[]{:T(128)S(6)} %select_n.50, f32[1,2,256,256]{3,2,1,0:T(8,128)} %collective-permute-done), kind=kLoop, calls=%fused_computation.45 | loop fusion | bytes 1048580 | tf_op jit(solution)/shard_map/dynamic_update_slice | solution.py:61
  31.4 0.0 collective-permute-done.1
  31.4 1.1 %bitcast_dynamic-update-slice_fusion = f32[4,1,2,256,256]{4,3,0,2,1:T(8,128)S(1)} fusion(f32[4,1,2,256,256]{4,3,0,2,1:T(8,128)S(1)} %bitcast_dynamic-update-slice_fusion.1, s32[]{:T(128)S(6)} %select_n.52, f32[1,2,256,256]{3,2,1,0:T(8,128)} %collective-permute-done.1), kind=kLoop, calls=%fused_computation.44 | loop fusion | bytes 1048580 | tf_op jit(solution)/shard_map/dynamic_update_slice | solution.py:66
  32.5 11.1 %collective-permute-done.2 = f32[1,2,256,256]{3,2,1,0:T(8,128)} collective-permute-done((f32[1,2,256,256]{3,2,1,0:T(8,128)}, f32[1,2,256,256]{3,2,1,0:T(8,128)}, u32[]{:S(2)}, u32[]{:S(2)}) %collective-permute-start.2) | collective-permute-done | bytes 524320 | tf_op jit(solution)/shard_map/ppermute | solution.py:60
  43.6 1.1 %bitcast_dynamic-update-slice_fusion.2 = f32[4,1,2,256,256]{4,3,0,2,1:T(8,128)S(1)} fusion(f32[4,1,2,256,256]{4,3,0,2,1:T(8,128)S(1)} %bitcast_dynamic-update-slice_fusion, s32[]{:T(128)S(6)} %select_n.54, f32[1,2,256,256]{3,2,1,0:T(8,128)} %collective-permute-done.2), kind=kLoop, calls=%fused_computation.46 | loop fusion | bytes 1048580 | tf_op jit(solution)/shard_map/dynamic_update_slice | solution.py:61
  44.7 0.5 broadcast_select_fusion
  45.2 0.2 fusion.42
  45.4 0.7 fusion.12
  46.1 0.7 fusion.13
  46.7 0.7 convolution_add_fusion
  47.4 0.7 convolution_subtract_fusion
  48.1 0.4 fusion.29
  48.4 0.4 fusion.28
  48.8 0.4 convolution_subtract_fusion.4
  49.2 0.3 fusion.37
  49.5 0.3 fusion.36
  49.8 0.2 fusion.43
  50.0 0.7 fusion.10
  50.7 0.7 fusion.11
  51.4 0.7 convolution_add_fusion.1
  52.0 0.7 convolution_subtract_fusion.1
  52.7 0.4 fusion.27
  53.1 0.4 fusion.26
  53.5 0.4 convolution_add_fusion.7
  53.9 0.0 copy-start.2
  53.9 0.4 convolution_subtract_fusion.7
  54.3 0.6 fusion.24
  54.9 0.6 fusion.22
  55.5 0.6 convolution_subtract_fusion.6
  56.1 0.0 copy-done.2
  56.1 0.6 fusion.14
  56.7 0.8 fusion.18
  57.5 0.4 convolution_add_fusion.5
  57.9 0.3 convolution_add_fusion.3
  58.2 0.3 convolution_subtract_fusion.3
  58.5 0.6 convolution_add_fusion.6
  59.1 0.6 convolution_add_fusion.4
  59.7 0.6 convolution_subtract_fusion.5
  60.3 0.0 copy-start.4
  60.3 0.4 fusion.45
  60.7 0.4 fusion.44
  61.1 1.0 %select_reduce_fusion = (f32[]{:T(128)}, f32[256,256]{1,0:T(8,128)S(1)}) fusion(f32[256,256]{1,0:T(8,128)S(1)} %fusion.45, f32[256,256]{1,0:T(8,128)S(1)} %convolution_add_fusion.4, f32[256,256]{1,0:T(8,128)S(1)} %convolution_subtract_fusion.3), kind=kOutput, calls=%fused_computation.72 | convolution fusion | flops 201588736 | bytes 1048580 | tf_op jit(solution)/shard_map/dot_general | solution.py:13
  62.0 1.0 %select_reduce_fusion.1 = (f32[]{:T(128)}, f32[256,256]{1,0:T(8,128)S(1)}) fusion(f32[256,256]{1,0:T(8,128)S(1)} %fusion.44, f32[256,256]{1,0:T(8,128)S(1)} %convolution_add_fusion.4, f32[256,256]{1,0:T(8,128)S(1)} %convolution_add_fusion.3), kind=kOutput, calls=%fused_computation.73 | convolution fusion | flops 201588736 | bytes 1048580 | tf_op jit(solution)/shard_map/dot_general | solution.py:10
  63.1 0.0 copy-start.3
  63.1 0.0 copy-done.4
  63.1 5.0 %convolution_bitcast_fusion = f32[4]{0:T(128)S(1)} fusion(f32[4,256,256]{2,1,0:T(8,128)S(1)} %copy-done.4, f32[256,256,1]{1,0,2:T(8,128)S(1)} %bitcast.157), kind=kOutput, calls=%fused_computation.16 | convolution fusion | flops 3145728 | bytes 1310736 | tf_op jit(solution)/shard_map/mkab,jab->mkj/dot_general | solution.py:83
  68.1 5.0 %convolution_bitcast_fusion.2 = f32[4]{0:T(128)S(1)} fusion(f32[4,256,256]{2,1,0:T(8,128)S(1)} %copy-done.4, f32[256,256,1]{1,0,2:T(8,128)S(1)} %bitcast.159), kind=kOutput, calls=%fused_computation.18 | convolution fusion | flops 3145728 | bytes 1310736 | tf_op jit(solution)/shard_map/mkab,jab->mkj/dot_general | solution.py:86
  73.1 0.0 copy-done.3
  73.1 5.6 %fusion.5 = f32[4]{0:T(128)S(1)} fusion(f32[4]{0:T(128)S(1)} %convolution_bitcast_fusion, f32[4,256,256]{2,1,0:T(8,128)S(1)} %copy-done.3, f32[256,256,1]{1,0,2:T(8,128)S(1)} %bitcast.160, f32[]{:T(128)} %get-tuple-element.15), kind=kOutput, calls=%fused_computation.25 | convolution fusion | flops 3145736 | bytes 1310756 | tf_op jit(solution)/shard_map/mkab,jab->mkj/dot_general | solution.py:81
  78.6 5.7 %fusion.3 = f32[1,4]{1,0:T(1,128)S(1)} fusion(f32[4]{0:T(128)S(1)} %fusion.5, f32[4]{0:T(128)S(1)} %convolution_bitcast_fusion.2, f32[4,256,256]{2,1,0:T(8,128)S(1)} %copy-done.3, f32[256,256,1]{1,0,2:T(8,128)S(1)} %bitcast.158, f32[]{:T(128)} %get-tuple-element.17), kind=kOutput, calls=%fused_computation.23 | convolution fusion | flops 3145740 | bytes 1310772 | tf_op jit(solution)/shard_map/mkab,jab->mkj/dot_general | solution.py:84
  84.3 5.6 %psum.7 = f32[1,4]{1,0:T(1,128)S(1)} all-reduce(f32[1,4]{1,0:T(1,128)S(1)} %fusion.3), channel_id=1, replica_groups=mesh['group'=2,'tm'=4,'member'=2,'sub'=2] {'member','sub'}, use_global_device_ids=true, to_apply=%region_2.3 | all-reduce | flops 4 | bytes 32 | tf_op jit(solution)/shard_map/psum | solution.py:89
  89.9 0.5 broadcast_multiply_fusion
  (3 shorter events, 0.1 us)
Async XLA Ops:
  0.0 5.2 %copy-start = (f32[1,1,2,256,256]{4,3,2,1,0:T(8,128)S(1)}, f32[1,1,2,256,256]{4,3,2,1,0:T(8,128)}, u32[]{:S(2)}) copy-start(f32[1,1,2,256,256]{4,3,2,1,0:T(8,128)} %param.3) | copy-start | bytes 1572868
  0.0 31.4 %collective-permute-start.1 = (f32[1,2,256,256]{3,2,1,0:T(8,128)}, f32[1,2,256,256]{3,2,1,0:T(8,128)}, u32[]{:S(2)}, u32[]{:S(2)}) collective-permute-start(f32[1,2,256,256]{3,2,1,0:T(8,128)} %bitcast.155), channel_id=1, source_target_pairs={{0,12},{4,0},{8,4},{12,8},{1,13},{5,1},{9,5},{13,9},{2,14},{6,2},{... | collective-permute-start | bytes 1572872 | tf_op jit(solution)/shard_map/ppermute | solution.py:65
  5.1 23.6 %collective-permute-start = (f32[1,2,256,256]{3,2,1,0:T(8,128)}, f32[1,2,256,256]{3,2,1,0:T(8,128)}, u32[]{:S(2)}, u32[]{:S(2)}) collective-permute-start(f32[1,2,256,256]{3,2,1,0:T(8,128)} %bitcast.156), channel_id=1, source_target_pairs={{0,4},{4,8},{8,12},{12,0},{1,5},{5,9},{9,13},{13,1},{2,6},{6,10},{... | collective-permute-start | bytes 1572872 | tf_op jit(solution)/shard_map/ppermute | solution.py:60
  5.1 1.6 %copy-start.1 = (f32[4,2,256,256]{3,2,1,0:T(8,128)S(1)}, f32[4,2,256,256]{3,2,1,0:T(8,128)}, u32[]{:S(2)}) copy-start(f32[4,2,256,256]{3,2,1,0:T(8,128)} %param.4) | copy-start | bytes 6291460
  28.7 14.9 %collective-permute-start.2 = (f32[1,2,256,256]{3,2,1,0:T(8,128)}, f32[1,2,256,256]{3,2,1,0:T(8,128)}, u32[]{:S(2)}, u32[]{:S(2)}) collective-permute-start(f32[1,2,256,256]{3,2,1,0:T(8,128)} %collective-permute-done), channel_id=1, source_target_pairs={{0,4},{4,8},{8,12},{12,0},{1,5},{5,9},{9,13},{13,1},{2,6},{6,10},{... | collective-permute-start | bytes 1572872 | tf_op jit(solution)/shard_map/ppermute | solution.py:60
  53.9 2.2 %copy-start.2 = (f32[2,256,256]{2,1,0:T(8,128)S(1)}, f32[2,256,256]{2,1,0:T(8,128)}, u32[]{:S(2)}) copy-start(f32[2,256,256]{2,1,0:T(8,128)} %param.5) | copy-start | bytes 1572868
  60.3 2.8 %copy-start.4 = (f32[4,256,256]{2,1,0:T(8,128)S(1)}, f32[4,256,256]{2,1,0:T(8,128)}, u32[]{:S(2)}) copy-start(f32[4,256,256]{2,1,0:T(8,128)} %get-tuple-element.8) | copy-start | bytes 3145732
  63.1 10.0 %copy-start.3 = (f32[4,256,256]{2,1,0:T(8,128)S(1)}, f32[4,256,256]{2,1,0:T(8,128)}, u32[]{:S(2)}) copy-start(f32[4,256,256]{2,1,0:T(8,128)} %get-tuple-element.7) | copy-start | bytes 3145732
